TPU v7x, 32 devices: a whole 2x2x4 slice. The times are simulated.
32 devices in a mesh: groups: 2 (over y), rows: 4 (over z), cols: 4 (over x, core).
Axes of the slice: x: 2, y: 2, z: 4, core: 2. Of those that a mesh axis runs over, the one named last changes fastest.
Arguments:
- points: bfloat16 [6144, 128], P(('groups', 'rows', 'cols')), parts along dimension 0, as said below
- solution: float32 [6144, 128], P(('groups', 'rows', 'cols')), parts along dimension 0, may hold values from -6 to 6
- targets: float32 [6144, 128], P(('groups', 'rows', 'cols')), parts along dimension 0, may hold values from -40 to 40, as said below
- inducing: int32 [2048], P('groups'), parts along dimension 0, may hold values from 0 to 3071, as said below
- woodbury_inverse: float32 [2048, 1024], P('groups'), parts along dimension 0, may hold values from -1 to 7, as said below
Outputs:
- new_solution: float32 [6144, 128], P(('groups', 'rows', 'cols')), parts along dimension 0
- residual: float32 [6144, 128], P(('groups', 'rows', 'cols')), parts along dimension 0
- relative_norm: float32 [256], P('groups'), parts along dimension 0
There are 2 independent parts, one for each index of `groups`. A program takes and returns all parts, laid end to end along the dimension named above; each array names one. Nothing has to cross between parts.
Inputs may be any that keep to these rules, and one draw needn't show every extreme that they name: `points`: input locations. targets of each right-hand side have their own scale. `inducing`: indices into this problem's points. `woodbury_inverse`: symmetric.
All inputs are finite; a program needn't handle non-finite values.
Results may differ from a plain program's by a relative error of at most 0.0031.
Values may be sent and summed in bfloat16 or wider, within the bound.
No kernel may reach another device: no remote copies, remote signals or barrier semaphores. Data moves between devices by JAX's collectives and lax.ppermute only.
A program may use at most 64 MiB of HBM per device.

v0:
```python
import jax
import jax.numpy as jnp
from jax import lax
from jax.sharding import PartitionSpec as P

F = 128
noise_level = 0.5
COLUMN_CHUNK = 3072


def square_norms(values):
    return jnp.sum(jnp.square(values.astype(jnp.float32)), axis=1)


def rbf_tile(left_x, left_sq, right_x, right_sq, gamma):
    inner = lax.dot_general(
        left_x, right_x, (((1,), (1,)), ((), ())), preferred_element_type=jnp.float32
    )
    return jnp.exp(-gamma * (left_sq[:, None] + right_sq[None, :] - 2.0 * inner)).astype(
        jnp.bfloat16
    )


def kernel_product(own_x, own_sq, all_x, all_sq, all_v, gamma):
    total = all_x.shape[0]
    chunk = min(COLUMN_CHUNK, total)
    if total % chunk != 0:
        chunk = total
    steps = total // chunk

    def piece(start):
        x = lax.dynamic_slice_in_dim(all_x, start, chunk, 0)
        s = lax.dynamic_slice_in_dim(all_sq, start, chunk, 0)
        v = lax.dynamic_slice_in_dim(all_v, start, chunk, 0)
        k = rbf_tile(own_x, own_sq, x, s, gamma)
        return jnp.dot(k, v, preferred_element_type=jnp.float32)

    if steps == 1:
        return piece(0)

    def body(i, acc):
        return acc + piece(i * chunk)

    init = jnp.zeros((own_x.shape[0], all_v.shape[1]), jnp.float32)
    return lax.fori_loop(0, steps, body, init)


def local(points, solution, targets, inducing, woodbury_inverse):
    gamma = 2.5 / F
    solution_b = solution.astype(jnp.bfloat16)
    packed = jnp.concatenate([points, solution_b], axis=1)
    gathered = lax.all_gather(packed, ("rows", "cols"), axis=0, tiled=True)
    all_x = gathered[:, :F]
    all_v = gathered[:, F:]
    all_sq = square_norms(all_x)
    own_sq = square_norms(points)
    kp = kernel_product(points, own_sq, all_x, all_sq, all_v, gamma)
    residual = targets - kp - noise_level * solution
    centers = jnp.take(all_x, inducing, axis=0)
    cross = rbf_tile(points, own_sq, centers, square_norms(centers), gamma)
    residual_b = residual.astype(jnp.bfloat16)
    projected_local = lax.dot_general(
        cross, residual_b, (((0,), (0,)), ((), ())), preferred_element_type=jnp.float32
    )
    res_local = jnp.sum(residual * residual, axis=0)
    tar_local = jnp.sum(targets * targets, axis=0)
    stacked = jnp.concatenate([projected_local, res_local[None], tar_local[None]], axis=0)
    summed = lax.psum(stacked, ("rows", "cols"))
    m = projected_local.shape[0]
    projected = summed[:m]
    res_sq = summed[m]
    tar_sq = summed[m + 1]
    weights = jnp.dot(woodbury_inverse, projected, precision=lax.Precision.HIGHEST)
    correction = jnp.dot(cross, weights.astype(jnp.bfloat16), preferred_element_type=jnp.float32)
    new_solution = solution + (residual - correction) / noise_level
    relative_norm = jnp.sqrt(res_sq / (tar_sq + 1e-06))
    return (new_solution, residual, relative_norm)


def solution(mesh):
    return jax.shard_map(
        local,
        mesh=mesh,
        in_specs=(
            P(("groups", "rows", "cols"), None),
            P(("groups", "rows", "cols"), None),
            P(("groups", "rows", "cols"), None),
            P("groups"),
            P("groups", None),
        ),
        out_specs=(
            P(("groups", "rows", "cols"), None),
            P(("groups", "rows", "cols"), None),
            P("groups"),
        ),
        check_vma=False,
    )
```

profile of v0, /device:TPU:0, one launch (start us, length us, event | category | flops | bytes accessed | tf_op | source)
XLA Modules:
  0.0 167.1 jit_solution(9886940378741417680)
XLA Ops:
  7.2 0.0 all-gather.2.cloned.1.call-start
  7.2 0.9 convert_element_type.26
  8.1 0.0 copy-start.3
  8.1 1.5 pad_maximum_fusion
  9.6 0.0 all-gather.2.cloned.1.call-update
  9.7 0.0 all-reduce.2.cloned.1.call-start
  9.7 0.9 multiply_reduce_fusion.4
  10.6 0.9 multiply_reduce_fusion.2
  11.6 0.7 compare_and_fusion
  12.3 0.7 fusion.23
  12.9 40.2 %all-gather.2.cloned.1.call-done = bf16[3072,256]{1,0:T(8,128)(2,1)} async-done(((bf16[192,256]{1,0:T(8,128)(2,1)}), bf16[3072,256]{1,0:T(8,128)(2,1)}) %all-gather.2.cloned.1.call-update) | async-done | bytes 1572880 | tf_op jit(solution)/shard_map/all_gather | solution.py:52
  53.2 0.0 slice-start
  53.2 1.1 slice-done
  54.3 0.0 copy-start
  54.3 0.0 copy-start.1
  54.3 0.0 copy-start.4
  54.3 3.2 %gather_fusion = bf16[1024,128]{1,0:T(8,128)(2,1)S(1)} fusion(bf16[3072,128]{1,0:T(8,128)(2,1)S(1)} %slice-done, s32[1024]{0:T(1024)S(1)} %fusion.23), kind=kCustom, calls=%fused_computation | custom fusion | bytes 528384 | tf_op jit(solution)/shard_map/jit(_take)/gather | solution.py:59
  57.5 0.4 multiply_reduce_fusion.1
  57.9 0.0 copy-done.3
  57.9 0.5 fusion.10
  58.4 0.0 copy-done
  58.4 0.5 multiply_reduce_fusion
  58.9 0.0 copy-done.1
  58.9 0.0 copy-done.4
  58.9 1.0 multiply_reduce_fusion.3
  59.9 0.0 copy-start.2
  59.9 0.3 fusion.21
  60.2 1.5 concatenate.7
  61.7 0.0 all-reduce.2.cloned.1.call-update
  61.7 89.5 %all-reduce.2.cloned.1.call-done = f32[1026,128]{1,0:T(8,128)} async-done(((f32[1026,128]{1,0:T(8,128)}), f32[1026,128]{1,0:T(8,128)}) %all-reduce.2.cloned.1.call-update) | async-done | bytes 525328 | tf_op jit(solution)/shard_map/psum | solution.py:68
  151.2 6.8 %convolution_convert_fusion = bf16[128,1024]{1,0:T(8,128)(2,1)S(1)} fusion(f32[1024,1024]{1,0:T(8,128)} %param.9, f32[1026,128]{1,0:T(8,128)} %all-reduce.2.cloned.1.call-done), kind=kOutput, calls=%fused_computation.15 | convolution fusion | flops 1610743808 | bytes 4980736 | tf_op jit(solution)/shard_map/dot_general | solution.py:73
  158.1 0.0 copy-done.2
  158.1 0.9 fusion.18
  159.0 1.3 sqrt_bitcast_fusion
Async XLA Ops:
  7.2 46.0 %all-gather.2.cloned.1.call-start = ((), (), s32[]{:S(2)}) async-start(), calls=%async_computation | async-start | bytes 1671168 | tf_op jit(solution)/shard_map/all_gather | solution.py:52
  8.1 49.8 %copy-start.3 = (bf16[192,128]{1,0:T(8,128)(2,1)S(1)}, bf16[192,128]{1,0:T(8,128)(2,1)}, u32[]{:S(2)}) copy-start(bf16[192,128]{1,0:T(8,128)(2,1)} %param.5) | copy-start | bytes 147460
  9.7 141.6 %all-reduce.2.cloned.1.call-start = ((), (), s32[]{:S(2)}) async-start(), calls=%async_computation.1 | async-start | bytes 1056768 | tf_op jit(solution)/shard_map/psum | solution.py:68
  53.2 1.1 slice-start
  54.3 4.1 %copy-start = (bf16[3072,256]{1,0:T(8,128)(2,1)S(1)}, bf16[3072,256]{1,0:T(8,128)(2,1)}, u32[]{:S(2)}) copy-start(bf16[3072,256]{1,0:T(8,128)(2,1)} %all-gather.2.cloned.1.call-done) | copy-start | bytes 4718596
  54.3 4.5 %copy-start.1 = (f32[192,128]{1,0:T(8,128)S(1)}, f32[192,128]{1,0:T(8,128)}, u32[]{:S(2)}) copy-start(f32[192,128]{1,0:T(8,128)} %param.6) | copy-start | bytes 294916
  54.3 4.6 %copy-start.4 = (f32[192,128]{1,0:T(8,128)S(1)}, f32[192,128]{1,0:T(8,128)}, u32[]{:S(2)}) copy-start(f32[192,128]{1,0:T(8,128)} %param.7) | copy-start | bytes 294916
  59.9 98.2 %copy-start.2 = (f32[192,128]{1,0:T(8,128)}, f32[192,128]{1,0:T(8,128)S(1)}, u32[]{:S(2)}) copy-start(f32[192,128]{1,0:T(8,128)S(1)} %get-tuple-element.4) | copy-start | bytes 294916
Sparse Core Ops, SparseCore 0:
  10.8 42.3 all-gather.1
  61.9 89.3 all-reduce.1
where the time goes:
time: 168 us; the launch traced here: 167 us
  waiting for transfers between devices  130 us (77%)
  between operations  14.1 us (8%)
  matrix products  9.53 us (6%)
  other arithmetic  7.78 us (5%)
  local copies, waits for them, and re-layouts  5.84 us (3%)
    psum x1, waiting for transfers between devices, local(): summed = lax.psum(stacked, ('rows', 'cols'))  89.5 us
    all_gather x1, waiting for transfers between devices, local(): gathered = lax.all_gather(packed, ('rows', 'cols'), axis=0, tiled=True)  40.2 us
    dot_general x1, matrix products, local(): jnp.dot(woodbury_inverse, projected, precision=lax.Precision.HIGHEST)  6.82 us
  transfers between devices with their start and end apart: 2, of which 2 were waited for; matrix products, arithmetic and copies ran while one was open for 2% of the time, Pallas kernels for 0%

commit v1 on v0

--- a/solution.py
+++ b/solution.py
@@ -65,7 +65,7 @@
     res_local = jnp.sum(residual * residual, axis=0)
     tar_local = jnp.sum(targets * targets, axis=0)
     stacked = jnp.concatenate([projected_local, res_local[None], tar_local[None]], axis=0)
-    summed = lax.psum(stacked, ("rows", "cols"))
+    summed = jnp.sum(lax.all_gather(stacked, ("rows", "cols")), axis=0)
     m = projected_local.shape[0]
     projected = summed[:m]
     res_sq = summed[m]

time: 168 us -> 155 us (0.923)
  waiting for transfers between devices: 130 us -> 114 us
  other arithmetic: 7.78 us -> 10.9 us
    psum x1 -> x0, waiting for transfers between devices: 89.5 us -> none  [local(): summed = lax.psum(stacked, ('rows', 'cols'))]
    all_gather x0 -> x1, waiting for transfers between devices: none -> 73.6 us  [local(): summed = jnp.sum(lax.all_gather(stacked, ('rows', 'cols')), axis=0)]
    reduce_sum x0 -> x1, other arithmetic: none -> 3.84 us  [local(): summed = jnp.sum(lax.all_gather(stacked, ('rows', 'cols')), axis=0)]
where the time goes in v1:
time: 155 us; the launch traced here: 154 us
  waiting for transfers between devices  114 us (74%)
  between operations  14.1 us (9%)
  other arithmetic  10.9 us (7%)
  matrix products  9.37 us (6%)
  local copies, waits for them, and re-layouts  5.87 us (4%)
    all_gather x1, waiting for transfers between devices, local(): summed = jnp.sum(lax.all_gather(stacked, ('rows', 'cols')), axis=0)  73.6 us
    all_gather x1, waiting for transfers between devices, local(): gathered = lax.all_gather(packed, ('rows', 'cols'), axis=0, tiled=True)  40.2 us
    dot_general x1, matrix products, local(): jnp.dot(woodbury_inverse, projected, precision=lax.Precision.HIGHEST)  6.67 us
    reduce_sum x1, other arithmetic, local(): summed = jnp.sum(lax.all_gather(stacked, ('rows', 'cols')), axis=0)  3.84 us
    gather x1, local copies, waits for them, and re-layouts, local(): centers = jnp.take(all_x, inducing, axis=0)  3.2 us
  transfers between devices with their start and end apart: 2, of which 2 were waited for; matrix products, arithmetic and copies ran while one was open for 2% of the time, Pallas kernels for 0%

profile of v1, /device:TPU:0, one launch (start us, length us, event | category | flops | bytes accessed | tf_op | source)
XLA Modules:
  0.0 154.1 jit_solution(15783901470251403249)
XLA Ops:
  7.2 0.0 all-gather.5.cloned.1.call-start
  7.2 0.9 convert_element_type.26
  8.1 0.0 copy-start.3
  8.1 1.5 pad_maximum_fusion
  9.6 0.0 all-gather.5.cloned.1.call-update
  9.7 0.0 all-gather.7.cloned.1.call-start
  9.7 0.9 multiply_reduce_fusion.4
  10.6 0.9 multiply_reduce_fusion.2
  11.6 0.7 compare_and_fusion
  12.3 0.7 fusion.23
  12.9 40.2 %all-gather.5.cloned.1.call-done = bf16[3072,256]{1,0:T(8,128)(2,1)} async-done(((bf16[192,256]{1,0:T(8,128)(2,1)}), bf16[3072,256]{1,0:T(8,128)(2,1)}) %all-gather.5.cloned.1.call-update) | async-done | bytes 1572880 | tf_op jit(solution)/shard_map/all_gather | solution.py:52
  53.2 0.0 slice-start
  53.2 1.1 slice-done
  54.3 0.0 copy-start
  54.3 0.0 copy-start.1
  54.3 0.0 copy-start.4
  54.3 3.2 %gather_fusion = bf16[1024,128]{1,0:T(8,128)(2,1)S(1)} fusion(bf16[3072,128]{1,0:T(8,128)(2,1)S(1)} %slice-done, s32[1024]{0:T(1024)S(1)} %fusion.23), kind=kCustom, calls=%fused_computation | custom fusion | bytes 528384 | tf_op jit(solution)/shard_map/jit(_take)/gather | solution.py:59
  57.5 0.4 multiply_reduce_fusion.1
  57.9 0.0 copy-done.3
  57.9 0.5 fusion.10
  58.4 0.0 copy-done
  58.4 0.5 multiply_reduce_fusion
  58.9 0.0 copy-done.1
  58.9 0.0 copy-done.4
  58.9 1.0 multiply_reduce_fusion.3
  59.9 0.0 copy-start.2
  59.9 0.3 fusion.21
  60.2 1.5 concatenate.7
  61.7 0.0 all-gather.7.cloned.1.call-update
  61.8 73.6 %all-gather.7.cloned.1.call-done = f32[16,1026,128]{2,1,0:T(8,128)} async-done(((f32[1,1026,128]{2,1,0:T(8,128)}), f32[16,1026,128]{2,1,0:T(8,128)}) %all-gather.7.cloned.1.call-update) | async-done | bytes 8405008 | tf_op jit(solution)/shard_map/all_gather | solution.py:68
  135.3 3.8 %reduce_sum.59 = f32[1026,128]{1,0:T(8,128)S(1)} reduce(f32[16,1026,128]{2,1,0:T(8,128)} %all-gather.7.cloned.1.call-done, f32[]{:T(128)} %constant.9.clone.1), dimensions={0}, to_apply=%region_5.6 | reduce | flops 1969920 | bytes 8930308 | tf_op jit(solution)/shard_map/reduce_sum | solution.py:68
  139.2 0.5 sqrt_bitcast_fusion
  139.7 6.7 %convolution_convert_fusion = bf16[128,1024]{1,0:T(8,128)(2,1)S(1)} fusion(f32[1024,1024]{1,0:T(8,128)} %param.9, f32[1026,128]{1,0:T(8,128)S(1)} %reduce_sum.59), kind=kOutput, calls=%fused_computation.15 | convolution fusion | flops 1610743808 | bytes 4980736 | tf_op jit(solution)/shard_map/dot_general | solution.py:73
  146.4 0.0 copy-done.2
  146.4 0.9 fusion.18
Async XLA Ops:
  7.2 46.0 %all-gather.5.cloned.1.call-start = ((), (), s32[]{:S(2)}) async-start(), calls=%async_computation | async-start | bytes 1671168 | tf_op jit(solution)/shard_map/all_gather | solution.py:52
  8.1 49.8 %copy-start.3 = (bf16[192,128]{1,0:T(8,128)(2,1)S(1)}, bf16[192,128]{1,0:T(8,128)(2,1)}, u32[]{:S(2)}) copy-start(bf16[192,128]{1,0:T(8,128)(2,1)} %param.5) | copy-start | bytes 147460
  9.7 125.7 %all-gather.7.cloned.1.call-start = ((), (), s32[]{:S(2)}) async-start(), calls=%async_computation.1 | async-start | bytes 8982528 | tf_op jit(solution)/shard_map/all_gather | solution.py:68
  53.2 1.1 slice-start
  54.3 4.1 %copy-start = (bf16[3072,256]{1,0:T(8,128)(2,1)S(1)}, bf16[3072,256]{1,0:T(8,128)(2,1)}, u32[]{:S(2)}) copy-start(bf16[3072,256]{1,0:T(8,128)(2,1)} %all-gather.5.cloned.1.call-done) | copy-start | bytes 4718596
  54.3 4.5 %copy-start.1 = (f32[192,128]{1,0:T(8,128)S(1)}, f32[192,128]{1,0:T(8,128)}, u32[]{:S(2)}) copy-start(f32[192,128]{1,0:T(8,128)} %param.6) | copy-start | bytes 294916
  54.3 4.6 %copy-start.4 = (f32[192,128]{1,0:T(8,128)S(1)}, f32[192,128]{1,0:T(8,128)}, u32[]{:S(2)}) copy-start(f32[192,128]{1,0:T(8,128)} %param.7) | copy-start | bytes 294916
  59.9 86.5 %copy-start.2 = (f32[192,128]{1,0:T(8,128)}, f32[192,128]{1,0:T(8,128)S(1)}, u32[]{:S(2)}) copy-start(f32[192,128]{1,0:T(8,128)S(1)} %get-tuple-element.4) | copy-start | bytes 294916
Sparse Core Ops, SparseCore 0:
  10.8 42.3 all-gather.4
  61.9 73.3 all-gather.6
